TPU v7x, 256 devices: a whole 4x4x8 slice. The times are simulated.
256 devices in a mesh: row: 32 (over z, x_lo, core), col: 8 (over y, x_hi).
Axes of the slice: x: 4 (x_hi: 2, x_lo: 2; x = x_hi * 2 + x_lo), y: 4, z: 8, core: 2. Of those that a mesh axis runs over, the one named last changes fastest.
Arguments:
- grad_out: bfloat16 [4096, 8192], P('row', 'col'), may hold values from -6 to 6
- weight: bfloat16 [28672, 8192], P('row', 'col'), may hold values from -0.0625 to 0.0625
Outputs:
- grad_in: bfloat16 [4096, 28672], P('col', 'row')
All inputs are finite; a program needn't handle non-finite values.
Results may differ from a plain program's by a relative error of at most 0.015.
Values may be sent and summed in bfloat16 or wider, within the bound.
No kernel may reach another device: no remote copies, remote signals or barrier semaphores. Data moves between devices by JAX's collectives and lax.ppermute only.
A program may use at most 128 MiB of HBM per device.

v0:
```python
import jax
import jax.numpy as jnp
from jax import lax
from jax.sharding import Mesh, PartitionSpec as P


def contract_last(left_side, right_side):
    return lax.dot_general(
        left_side, right_side, (((1,), (1,)), ((), ())), preferred_element_type=jnp.float32
    )


def body(grad_out, weight):
    n_col = lax.axis_size("col")
    n_core = lax.axis_size("core")
    both = lax.all_gather(weight, "core", axis=0, tiled=True)
    gathered = lax.all_gather(grad_out, "rz", axis=0, tiled=True)
    rounded = contract_last(gathered, both).astype(jnp.bfloat16)
    blocks = rounded.reshape(n_col, rounded.shape[0] // n_col, rounded.shape[1])
    received = lax.all_to_all(blocks, "col", 0, 0, tiled=True)
    summed = received.astype(jnp.float32).sum(0).astype(jnp.bfloat16)
    rows, width = (summed.shape[0], weight.shape[0])
    by_owner = summed.reshape(rows, n_core, width).transpose(1, 0, 2)
    mine = lax.all_to_all(by_owner, "core", 0, 0, tiled=True)
    per_row = grad_out.shape[0]
    mine = mine.reshape(n_core, rows // per_row, per_row, width).transpose(1, 0, 2, 3)
    return mine.reshape(-1, width)


def solution(mesh):
    n_row, n_col = mesh.devices.shape
    fine = Mesh(mesh.devices.reshape(n_row // 2, 2, n_col), ("rz", "core", "col"))
    in_specs = (P(("rz", "core"), "col"), P(("rz", "core"), "col"))
    out_specs = P("col", ("rz", "core"))
    return jax.shard_map(body, mesh=fine, in_specs=in_specs, out_specs=out_specs, check_vma=False)
```

profile of v0, /device:TPU:1, one launch (start us, length us, event | category | flops | bytes accessed | tf_op | source)
XLA Modules:
  0.0 252.7 jit_solution(3287596444993253392)
XLA Ops:
  6.5 0.0 all-gather.5.cloned.1.call-start
  6.5 0.7 all-gather.5.cloned.1.call-update
  7.3 0.0 all-gather.3.cloned.1.call-start
  7.3 0.7 all-gather.3.cloned.1.call-update
  8.0 23.9 %all-gather.5.cloned.1.call-done = bf16[1792,1024]{1,0:T(8,128)(2,1)} async-done(((bf16[896,1024]{1,0:T(8,128)(2,1)}), bf16[1792,1024]{1,0:T(8,128)(2,1)}) %all-gather.5.cloned.1.call-update) | async-done | bytes 3670032 | tf_op jit(solution)/shard_map/all_gather | solution.py:16
  31.9 99.0 %all-gather.3.cloned.1.call-done = bf16[2048,1024]{1,0:T(8,128)(2,1)} async-done(((bf16[128,1024]{1,0:T(8,128)(2,1)}), bf16[2048,1024]{1,0:T(8,128)(2,1)}) %all-gather.3.cloned.1.call-update) | async-done | bytes 4194320 | tf_op jit(solution)/shard_map/all_gather | solution.py:17
  131.0 10.7 %convolution_convert_fusion = bf16[2048,1792]{1,0:T(8,128)(2,1)S(1)} fusion(bf16[2048,1024]{1,0:T(8,128)(2,1)} %all-gather.3.cloned.1.call-done, bf16[1792,1024]{1,0:T(8,128)(2,1)} %all-gather.5.cloned.1.call-done), kind=kOutput, calls=%fused_computation | convolution fusion | flops 7519862784 | bytes 15204352 | tf_op jit(solution)/shard_map/dot_general | solution.py:8
  141.6 90.8 %all_to_all.10 = bf16[8,256,1792]{2,1,0:T(8,128)(2,1)} all-to-all(bf16[8,256,1792]{2,1,0:T(8,128)(2,1)S(1)} %bitcast.10), channel_id=1, replica_groups=mesh['rz'=16,'core'=2,'col'=8] {'col'}, dimensions={0} | all-to-all | bytes 14680064 | tf_op jit(solution)/shard_map/all_to_all | solution.py:20
  232.5 4.6 %reduce_sum.12 = bf16[256,1792]{1,0:T(8,128)(2,1)S(1)} reduce(bf16[8,256,1792]{2,1,0:T(8,128)(2,1)} %all_to_all.10, bf16[]{:T(256)} %constant.2.clone.1), dimensions={0}, to_apply=%region_0.0 | reduce | flops 3211264 | bytes 8257538 | tf_op jit(solution)/shard_map/reduce_sum | solution.py:21
  237.1 0.5 copy.5
  237.6 6.6 %all_to_all.11 = bf16[2,256,896]{1,2,0:T(8,128)(2,1)S(1)} all-to-all(bf16[2,256,896]{1,2,0:T(8,128)(2,1)S(1)} %bitcast.11), channel_id=1, replica_groups=mesh['rz'=16,'core'=2,'col'=8] {'core'}, dimensions={0} | all-to-all | bytes 1835008 | tf_op jit(solution)/shard_map/all_to_all | solution.py:24
  244.2 0.6 copy.6
  244.8 1.0 copy.7
Async XLA Ops:
  6.5 25.4 %all-gather.5.cloned.1.call-start = ((), (), s32[]{:S(2)}) async-start(), calls=%async_computation.3 | async-start | bytes 5505024 | tf_op jit(solution)/shard_map/all_gather | solution.py:16
  7.3 123.7 %all-gather.3.cloned.1.call-start = ((), (), s32[]{:S(2)}) async-start(), calls=%async_computation.2 | async-start | bytes 4456448 | tf_op jit(solution)/shard_map/all_gather | solution.py:17
Sparse Core Ops, SparseCore 0:
  9.1 22.7 all-gather.4
  33.7 97.2 all-gather.2
where the time goes:
time: 253 us
  waiting for transfers between devices  124 us (49%)
  blocking collectives  97.5 us (39%)
  between operations  13.4 us (5%)
  matrix products  10.7 us (4%)
  other arithmetic  4.59 us (2%)
    all_gather x1, waiting for transfers between devices, body(): gathered = lax.all_gather(grad_out, 'rz', axis=0, tiled=True)  99 us
    all_to_all x1, blocking collectives, body(): received = lax.all_to_all(blocks, 'col', 0, 0, tiled=True)  90.8 us
    all_gather x1, waiting for transfers between devices, body(): both = lax.all_gather(weight, 'core', axis=0, tiled=True)  23.9 us
    dot_general x1, matrix products, contract_last(): lax.dot_general(left_side, right_side, (((1,), (1,)), ((), ())), preferre...  10.7 us
    all_to_all x1, blocking collectives, body(): mine = lax.all_to_all(by_owner, 'core', 0, 0, tiled=True)  6.62 us
  transfers between devices with their start and end apart: 2, of which 2 were waited for; matrix products, arithmetic and copies ran while one was open for 0% of the time, Pallas kernels for 0%

commit v1 on v0

--- a/solution.py
+++ b/solution.py
@@ -13,7 +13,14 @@
 def body(grad_out, weight):
     n_col = lax.axis_size("col")
     n_core = lax.axis_size("core")
-    both = lax.all_gather(weight, "core", axis=0, tiled=True)
+
+    def review_tiles(u):
+        current_block = lax.axis_size("core")
+        z1 = jnp.stack([u] * current_block)
+        main = lax.all_to_all(z1, concat_axis=0, axis_name="core", split_axis=0)
+        return jnp.concatenate(main, axis=0)
+
+    both = review_tiles(weight)
     gathered = lax.all_gather(grad_out, "rz", axis=0, tiled=True)
     rounded = contract_last(gathered, both).astype(jnp.bfloat16)
     blocks = rounded.reshape(n_col, rounded.shape[0] // n_col, rounded.shape[1])

time: 253 us -> 237 us (0.937)
  waiting for transfers between devices: 124 us -> 90.1 us
  blocking collectives: 97.5 us -> 108 us
  local copies, waits for them, and re-layouts: 2.12 us -> 5.14 us
    all_gather x1 -> x0, waiting for transfers between devices: 23.9 us -> none  [body(): both = lax.all_gather(weight, 'core', axis=0, tiled=True)]
    all_to_all x0 -> x1, blocking collectives: none -> 10.6 us  [review_tiles(): main = lax.all_to_all(z1, concat_axis=0, axis_name='core', split_axis=0)]
    all_gather x1, waiting for transfers between devices: 99 us -> 89.3 us  [body(): gathered = lax.all_gather(grad_out, 'rz', axis=0, tiled=True)]
    reshape x0 -> x1, local copies, waits for them, and re-layouts: none -> 3.55 us  [body(): blocks = rounded.reshape(n_col, rounded.shape[0] // n_col, rounded.shape[1])]
  transfers between devices with their start and end apart: 2 -> 1, of which waited for: 2 -> 1; matrix products, arithmetic and copies ran while one was open for 0% -> 1% of each run, Pallas kernels for 0% -> 0%
where the time goes in v1:
time: 237 us; the launch traced here: 236 us
  blocking collectives  108 us (46%)
  waiting for transfers between devices  90.1 us (38%)
  between operations  13.4 us (6%)
  matrix products  12.6 us (5%)
  other arithmetic  7.05 us (3%)
  local copies, waits for them, and re-layouts  5.14 us (2%)
    all_to_all x1, blocking collectives, body(): received = lax.all_to_all(blocks, 'col', 0, 0, tiled=True)  90.8 us
    all_gather x1, waiting for transfers between devices, body(): gathered = lax.all_gather(grad_out, 'rz', axis=0, tiled=True)  89.3 us
    dot_general x1, matrix products, contract_last(): lax.dot_general(left_side, right_side, (((1,), (1,)), ((), ())), preferre...  12.6 us
    all_to_all x1, blocking collectives, review_tiles(): main = lax.all_to_all(z1, concat_axis=0, axis_name='core', split_axis=0)  10.6 us
    all_to_all x1, blocking collectives, body(): mine = lax.all_to_all(by_owner, 'core', 0, 0, tiled=True)  6.62 us
  transfers between devices with their start and end apart: 1, of which 1 were waited for; matrix products, arithmetic and copies ran while one was open for 1% of the time, Pallas kernels for 0%

profile of v1, /device:TPU:1, one launch (start us, length us, event | category | flops | bytes accessed | tf_op | source)
XLA Modules:
  0.0 236.3 jit_solution(15932079477567392067)
XLA Ops:
  6.5 0.0 all-gather.2.cloned.1.call-start
  6.5 0.7 all-gather.2.cloned.1.call-update
  7.3 2.4 %pad_maximum_fusion = bf16[2,896,1024]{2,1,0:T(8,128)(2,1)S(1)} fusion(bf16[1,896,1024]{2,1,0:T(8,128)(2,1)} %bitcast.21), kind=kLoop, calls=%fused_computation.2 | loop fusion | flops 1835008 | bytes 5505024 | tf_op jit(solution)/shard_map/stack | solution.py:19
  9.6 10.6 %all_to_all.15 = bf16[2,896,1024]{2,1,0:T(8,128)(2,1)} all-to-all(bf16[2,896,1024]{2,1,0:T(8,128)(2,1)S(1)} %pad_maximum_fusion), channel_id=1, replica_groups=mesh['rz'=16,'core'=2,'col'=8] {'core'}, dimensions={0} | all-to-all | bytes 7340032 | tf_op jit(solution)/shard_map/all_to_all | solution.py:20
  20.2 89.3 %all-gather.2.cloned.1.call-done = bf16[2048,1024]{1,0:T(8,128)(2,1)} async-done(((bf16[128,1024]{1,0:T(8,128)(2,1)}), bf16[2048,1024]{1,0:T(8,128)(2,1)}) %all-gather.2.cloned.1.call-update) | async-done | bytes 4194320 | tf_op jit(solution)/shard_map/all_gather | solution.py:24
  109.6 12.6 %convolution_convert_fusion = bf16[1792,2048]{1,0:T(8,128)(2,1)} fusion(bf16[1792,1024]{1,0:T(8,128)(2,1)} %bitcast.19, bf16[2048,1024]{1,0:T(8,128)(2,1)} %all-gather.2.cloned.1.call-done), kind=kOutput, calls=%fused_computation | convolution fusion | flops 7519862784 | bytes 15204352 | tf_op jit(solution)/shard_map/dot_general | solution.py:8
  122.2 3.6 %copy.10 = bf16[224,8,8,256]{3,2,0,1:T(8,128)(2,1)S(1)} copy(bf16[224,8,8,256]{3,2,1,0:T(8,128)(2,1)} %bitcast.17) | data formatting | bytes 14680064 | tf_op jit(solution)/shard_map/reshape | solution.py:26
  125.7 90.8 %all_to_all.16 = bf16[8,256,1792]{1,2,0:T(8,128)(2,1)} all-to-all(bf16[8,256,1792]{1,2,0:T(8,128)(2,1)S(1)} %bitcast.16), channel_id=1, replica_groups=mesh['rz'=16,'core'=2,'col'=8] {'col'}, dimensions={0} | all-to-all | bytes 14680064 | tf_op jit(solution)/shard_map/all_to_all | solution.py:27
  216.6 4.7 %reduce_sum.12 = bf16[256,1792]{0,1:T(8,128)(2,1)S(1)} reduce(bf16[8,256,1792]{1,2,0:T(8,128)(2,1)} %all_to_all.16, bf16[]{:T(256)} %constant.2.clone.1), dimensions={0}, to_apply=%region_0.0 | reduce | flops 3211264 | bytes 8257538 | tf_op jit(solution)/shard_map/reduce_sum | solution.py:28
  221.2 6.6 %all_to_all.17 = bf16[2,256,896]{1,2,0:T(8,128)(2,1)S(1)} all-to-all(bf16[2,256,896]{1,2,0:T(8,128)(2,1)S(1)} %bitcast.18), channel_id=1, replica_groups=mesh['rz'=16,'core'=2,'col'=8] {'core'}, dimensions={0} | all-to-all | bytes 1835008 | tf_op jit(solution)/shard_map/all_to_all | solution.py:31
  227.9 0.6 copy.6
  228.5 1.0 copy.7
Async XLA Ops:
  6.5 103.1 %all-gather.2.cloned.1.call-start = ((), (), s32[]{:S(2)}) async-start(), calls=%async_computation.3 | async-start | bytes 4456448 | tf_op jit(solution)/shard_map/all_gather | solution.py:24
Sparse Core Ops, SparseCore 0:
  9.1 100.4 all-gather.1
